TPU v7x, 256 devices: a whole 4x4x8 slice. The times are simulated.
256 devices in a mesh: dp: 16 (over x, y_hi, core), mp: 16 (over y_lo, z).
Axes of the slice: x: 4, y: 4 (y_hi: 2, y_lo: 2; y = y_hi * 2 + y_lo), z: 8, core: 2. Of those that a mesh axis runs over, the one named last changes fastest.
Arguments:
- tokens: bfloat16 [4096, 4096], P('dp'), may hold values from -32 to 32
- weights: bfloat16 [4096, 2, 3, 4096], P('dp', None, None, 'mp'), may hold values from -1 to 1
- block_modality: int32 [32], replicated, may hold values from 0 to 1
- doc_ids: int32 [4096], replicated, may hold values from 0 to 31, never falling along the last dimension, each value on 1 to 1024 neighbouring positions
- grad_out: bfloat16 [4096, 4096], P('dp', 'mp'), may hold values from -6 to 6
Outputs:
- attended: bfloat16 [4096, 4096], P('dp', 'mp')
- grad_tokens: bfloat16 [4096, 4096], P('dp', 'mp')
- grad_weights: bfloat16 [4096, 2, 3, 4096], P('dp', None, None, 'mp')
Inputs may be any that keep to these rules, and one draw needn't show every extreme that they name: doc_ids never falls along the sequence; a document is a run of equal ids of at most 1024 tokens, and one document has exactly 1024.
All inputs are finite; a program needn't handle non-finite values.
Results may differ from a plain program's by a relative error of at most 0.025.
Values may be sent and summed in bfloat16 or wider, within the bound.
No kernel may reach another device: no remote copies, remote signals or barrier semaphores. Data moves between devices by JAX's collectives and lax.ppermute only.
A program may use at most 128 MiB of HBM per device.

v0:
```python
import jax
import jax.numpy as jnp
from jax import lax
from jax.sharding import PartitionSpec as P

HD = 128
BLOCK = 128
SPAN = 4


def shifted(block, axis, distance):
    devices = range(lax.axis_size(axis))
    route = [(i - distance, i) for i in devices if i - distance in devices]
    return lax.ppermute(block, axis, route)


def split_by_modality(rows, is_image):
    zeros = jnp.zeros_like(rows)
    text = jnp.where(is_image[:, None], zeros, rows)
    image = jnp.where(is_image[:, None], rows, zeros)
    return jnp.stack([text, image], axis=2).reshape(rows.shape[0], 2 * rows.shape[1])


def split_by_modality_major(rows, is_image):
    zeros = jnp.zeros_like(rows)
    text = jnp.where(is_image[:, None], zeros, rows)
    image = jnp.where(is_image[:, None], rows, zeros)
    return jnp.concatenate([text, image], axis=1)


def dp_ring(size):
    if size % 4:
        return list(range(size))
    chips = size // 2
    order = [2 * x for x in range(chips // 2)] + [2 * x + 1 for x in reversed(range(chips // 2))]
    return [2 * chip + core for chip in order for core in range(2)]


def ring_blocks(rows, ring, axis):
    shape = rows.shape
    blocks = rows.reshape(shape[:axis] + (len(ring), shape[axis] // len(ring)) + shape[axis + 1 :])
    return jnp.take(blocks, jnp.array(ring, jnp.int32), axis=axis).reshape(shape)


def on_device(tokens, weights, block_modality, doc_ids, grad_out):
    local_rows = tokens.shape[0]
    width_rows = weights.shape[0]
    head_width = weights.shape[3]
    head_count = head_width // HD
    dp_devices = lax.axis_size("dp")
    mp_devices = lax.axis_size("mp")
    local_blocks = local_rows // BLOCK
    front_pad = SPAN * local_rows
    window_len = front_pad + local_rows
    my_index = lax.axis_index("dp")
    scale_factor = HD ** (-0.5)
    token_image = jnp.repeat(block_modality, BLOCK) == 1
    my_image = lax.dynamic_slice_in_dim(token_image, my_index * local_rows, local_rows, 0)
    ring = dp_ring(dp_devices)
    inverse = [ring.index(k) for k in range(dp_devices)]
    flat_weights = (
        weights.reshape(width_rows, 2, 3 * head_width)
        .transpose(1, 0, 2)
        .reshape(2 * width_rows, 3 * head_width)
    )
    stacked_weights = lax.all_gather(
        flat_weights, "dp", axis=0, tiled=True, axis_index_groups=[ring]
    )
    columns = lax.all_to_all(tokens, "dp", split_axis=1, concat_axis=0, tiled=True)
    ring_columns = split_by_modality_major(
        ring_blocks(columns, ring, 0), ring_blocks(token_image, ring, 0)
    )
    ring_tokens = ring_blocks(tokens, ring, 1).reshape(local_rows, dp_devices, 1, width_rows)
    ring_tokens = jnp.concatenate(
        [
            jnp.where(my_image[:, None, None, None], jnp.zeros_like(ring_tokens), ring_tokens),
            jnp.where(my_image[:, None, None, None], ring_tokens, jnp.zeros_like(ring_tokens)),
        ],
        axis=2,
    ).reshape(local_rows, -1)
    stacked_weights, ring_columns, ring_tokens = lax.optimization_barrier(
        (stacked_weights, ring_columns, ring_tokens)
    )
    block_weights = stacked_weights.reshape(dp_devices, 2, width_rows, 3 * head_width)
    key_values = (
        jnp.dot(ring_tokens, stacked_weights[:, head_width:], preferred_element_type=jnp.float32)
        .astype(jnp.bfloat16)
        .reshape(local_rows, 2, head_count, HD)
    )
    received = []
    for distance in range(SPAN, 0, -1):
        received.append(shifted(key_values, "dp", distance))
    queries = (
        jnp.dot(ring_tokens, stacked_weights[:, :head_width], preferred_element_type=jnp.float32)
        .astype(jnp.bfloat16)
        .reshape(local_rows, head_count, HD)
    )
    window = jnp.concatenate(received + [key_values], 0)
    key_rows = window[:, 0]
    value_rows = window[:, 1]
    docs_pad = jnp.concatenate([jnp.full((front_pad,), -1, jnp.int32), doc_ids], 0)
    key_docs = lax.dynamic_slice_in_dim(docs_pad, my_index * local_rows, window_len, 0)
    query_docs = lax.dynamic_slice_in_dim(doc_ids, my_index * local_rows, local_rows, 0)
    offsets = jnp.arange(window_len, dtype=jnp.int32) - front_pad
    allowed = (key_docs[None, :] == query_docs[:, None]) & (
        offsets[None, :] <= jnp.arange(local_rows, dtype=jnp.int32)[:, None]
    )
    scores = (
        jnp.einsum("qhd,khd->hqk", queries, key_rows, preferred_element_type=jnp.float32)
        * scale_factor
    )
    scores = jnp.where(allowed[None], scores, -1e30)
    top_score = jnp.max(scores, axis=-1, keepdims=True)
    expos = jnp.where(allowed[None], jnp.exp(scores - top_score), 0.0)
    probs_f = expos / jnp.sum(expos, axis=-1, keepdims=True)
    probs = probs_f.astype(jnp.bfloat16)
    attended = jnp.einsum("hqk,khd->qhd", probs, value_rows, preferred_element_type=jnp.float32)
    attended = attended.astype(jnp.bfloat16).reshape(local_rows, head_width)
    upstream = grad_out.reshape(local_rows, head_count, HD)
    dprob = jnp.einsum("qhd,khd->hqk", upstream, value_rows, preferred_element_type=jnp.float32)
    row_delta = jnp.sum(probs_f * dprob, axis=-1, keepdims=True)
    dscore = (probs_f * (dprob - row_delta)).astype(jnp.bfloat16)
    grad_q = (
        jnp.einsum("hqk,khd->qhd", dscore, key_rows, preferred_element_type=jnp.float32)
        * scale_factor
    )
    grad_k = (
        jnp.einsum("hqk,qhd->khd", dscore, queries, preferred_element_type=jnp.float32)
        * scale_factor
    )
    grad_v = jnp.einsum("hqk,qhd->khd", probs, upstream, preferred_element_type=jnp.float32)
    window_grads = jnp.stack([grad_k, grad_v], 1)
    own_grads = window_grads[front_pad:]
    for distance in range(1, SPAN + 1):
        lower_edge = front_pad - distance * local_rows
        sent_block = window_grads[lower_edge : lower_edge + local_rows]
        own_grads = own_grads + shifted(sent_block.astype(jnp.bfloat16), "dp", -distance).astype(
            sent_block.dtype
        )
    dqkv = (
        jnp.concatenate([grad_q[:, None], own_grads], 1)
        .astype(jnp.bfloat16)
        .reshape(local_rows, 3 * head_width)
    )
    zeros = jnp.zeros_like(dqkv)
    parts = lax.dot_general(
        jnp.where(my_image[:, None], zeros, dqkv),
        block_weights[:, 0],
        (((1,), (2,)), ((), ())),
        preferred_element_type=jnp.float32,
    ) + lax.dot_general(
        jnp.where(my_image[:, None], dqkv, zeros),
        block_weights[:, 1],
        (((1,), (2,)), ((), ())),
        preferred_element_type=jnp.float32,
    )
    parts = jnp.take(
        parts.astype(jnp.bfloat16).transpose(1, 0, 2), jnp.array(inverse, jnp.int32), axis=0
    ).reshape(mp_devices, local_rows, -1)
    group_parts = lax.all_to_all(parts, "mp", split_axis=0, concat_axis=0, tiled=True)
    grad_tokens = jnp.sum(group_parts.astype(jnp.float32), axis=0).astype(jnp.bfloat16)
    gathered = lax.all_gather(dqkv[None], "dp", axis=0, tiled=True, axis_index_groups=[ring])
    weight_sum = lax.dot_general(
        ring_columns.reshape(dp_devices, local_rows, -1),
        gathered,
        (((0, 1), (0, 1)), ((), ())),
        preferred_element_type=jnp.float32,
    )
    grad_weights = (
        weight_sum.astype(jnp.bfloat16)
        .reshape(2, width_rows, 3 * head_width)
        .transpose(1, 0, 2)
        .reshape(width_rows, 2, 3, head_width)
    )
    return (attended, grad_tokens, grad_weights)


def solution(mesh):
    return jax.shard_map(
        on_device,
        mesh=mesh,
        in_specs=(P("dp", None), P("dp", None, None, "mp"), P(), P(), P("dp", "mp")),
        out_specs=(P("dp", "mp"), P("dp", "mp"), P("dp", None, None, "mp")),
        check_vma=False,
    )
```

profile of v0, /device:TPU:97, one launch (start us, length us, event | category | flops | bytes accessed | tf_op | source)
XLA Modules:
  0.0 262.4 jit_solution(9539630087630359603)
XLA Ops:
  10.6 3.3 %copy.77 = bf16[256,4096]{0,1:T(8,128)(2,1)S(1)} copy(bf16[256,4096]{1,0:T(8,128)(2,1)} %param.11) | data formatting | bytes 4194304 | tf_op args[0]
  13.9 2.5 copy.78
  16.4 7.7 %all-to-all-start = ((bf16[256,16,256]{2,0,1:T(8,128)(2,1)}), bf16[256,16,256]{2,0,1:T(8,128)(2,1)}, u32[]{:S(2)}, u32[]{:S(2)}) async-start(bf16[256,16,256]{2,0,1:T(8,128)(2,1)} %copy.78), calls=%async_computation | async-start | bytes 4194304 | tf_op jit(solution)/shard_map/all_to_all | solution.py:69
  24.4 2.5 gather_fusion.1
  28.1 2.3 pad_maximum_fusion.1
  30.4 6.4 %copy.80 = bf16[256,16,2,256]{0,3,2,1:T(8,128)(2,1)} copy(bf16[256,16,2,256]{3,0,1,2:T(8,128)(2,1)} %pad_maximum_fusion.1) | data formatting | bytes 8388608 | tf_op jit(solution)/shard_map/concatenate | solution.py:74
  37.3 30.9 %all-to-all-done = bf16[256,16,256]{2,0,1:T(8,128)(2,1)} async-done(((bf16[256,16,256]{2,0,1:T(8,128)(2,1)}), bf16[256,16,256]{2,0,1:T(8,128)(2,1)}, u32[]{:S(2)}, u32[]{:S(2)}) %all-to-all-start) | async-done | bytes 2097184 | tf_op jit(solution)/shard_map/all_to_all | solution.py:69
  72.7 2.4 pad_maximum_fusion
  75.0 36.4 %all-gather.3.cloned.1.call-done = bf16[8192,768]{1,0:T(8,128)(2,1)} async-done(((bf16[512,768]{1,0:T(8,128)(2,1)}), bf16[8192,768]{1,0:T(8,128)(2,1)}) %all-gather.3.cloned.1.call-update) | async-done | bytes 12582928 | tf_op jit(solution)/shard_map/all_gather | solution.py:66
  111.5 7.0 %fusion.15 = bf16[256,512]{1,0:T(8,128)(2,1)S(1)} fusion(bf16[256,8192]{0,1:T(8,128)(2,1)} %bitcast.99, bf16[8192,768]{1,0:T(8,128)(2,1)} %all-gather.3.cloned.1.call-done), kind=kOutput, calls=%fused_computation.40 | convolution fusion | flops 2147614720 | bytes 12845056 | tf_op jit(solution)/shard_map/dot_general | solution.py:86
  120.1 3.2 %collective-permute-start.1 = (bf16[256,2,2,128]{3,0,2,1:T(8,128)(2,1)S(1)}, bf16[256,2,2,128]{3,0,2,1:T(8,128)(2,1)S(1)}, u32[]{:S(2)}, u32[]{:S(2)}) collective-permute-start(bf16[256,2,2,128]{3,0,2,1:T(8,128)(2,1)S(1)} %copy.81), channel_id=1, source_target_pairs={{0,48},{16,64},{32,80},{48,96},{64,112},{80,128},{96,144},{112,160... | collective-permute-start | bytes 786440 | tf_op jit(solution)/shard_map/ppermute | solution.py:14
  123.3 4.8 %collective-permute-start.2 = (bf16[256,2,2,128]{3,0,2,1:T(8,128)(2,1)S(1)}, bf16[256,2,2,128]{3,0,2,1:T(8,128)(2,1)S(1)}, u32[]{:S(2)}, u32[]{:S(2)}) collective-permute-start(bf16[256,2,2,128]{3,0,2,1:T(8,128)(2,1)S(1)} %copy.81), channel_id=1, source_target_pairs={{0,32},{16,48},{32,64},{48,80},{64,96},{80,112},{96,128},{112,144}... | collective-permute-start | bytes 786440 | tf_op jit(solution)/shard_map/ppermute | solution.py:14
  128.1 4.7 %collective-permute-start.3 = (bf16[256,2,2,128]{3,0,2,1:T(8,128)(2,1)S(1)}, bf16[256,2,2,128]{3,0,2,1:T(8,128)(2,1)S(1)}, u32[]{:S(2)}, u32[]{:S(2)}) collective-permute-start(bf16[256,2,2,128]{3,0,2,1:T(8,128)(2,1)S(1)} %copy.81), channel_id=1, source_target_pairs={{0,16},{16,32},{32,48},{48,64},{64,80},{80,96},{96,112},{112,128},... | collective-permute-start | bytes 786440 | tf_op jit(solution)/shard_map/ppermute | solution.py:14
  132.8 5.2 %fusion.19 = bf16[256,256]{0,1:T(8,128)(2,1)S(1)} fusion(bf16[256,8192]{0,1:T(8,128)(2,1)} %bitcast.100, bf16[8192,768]{1,0:T(8,128)(2,1)} %all-gather.3.cloned.1.call-done), kind=kOutput, calls=%fused_computation.43 | convolution fusion | flops 1073807360 | bytes 8519680 | tf_op jit(solution)/shard_map/dot_general | solution.py:94
  139.3 2.6 fusion.33
  152.4 2.7 %collective-permute-done.7 = bf16[256,2,2,128]{0,3,2,1:T(8,128)(2,1)S(1)} collective-permute-done((bf16[256,2,2,128]{0,3,2,1:T(8,128)(2,1)S(1)}, bf16[256,2,2,128]{0,3,2,1:T(8,128)(2,1)S(1)}, u32[]{:S(2)}, u32[]{:S(2)}) %collective-permute-start.7) | collective-permute-done | bytes 262176 | tf_op jit(solution)/shard_map/ppermute | solution.py:14
  155.1 10.9 %collective-permute-done.6 = bf16[256,2,2,128]{0,3,2,1:T(8,128)(2,1)S(1)} collective-permute-done((bf16[256,2,2,128]{0,3,2,1:T(8,128)(2,1)S(1)}, bf16[256,2,2,128]{0,3,2,1:T(8,128)(2,1)S(1)}, u32[]{:S(2)}, u32[]{:S(2)}) %collective-permute-start.6) | collective-permute-done | bytes 262176 | tf_op jit(solution)/shard_map/ppermute | solution.py:14
  167.3 4.6 %fusion.3 = f32[256,16,256]{2,0,1:T(8,128)S(1)} fusion(bf16[256,768,1]{0,1,2:T(8,128)(2,1)S(1)} %bitcast.109, bf16[16,2,256,768]{3,2,1,0:T(8,128)(2,1)} %bitcast.102), kind=kOutput, calls=%fused_computation.8 | convolution fusion | flops 1610612736 | bytes 10878976 | tf_op jit(solution)/shard_map/dot_general | solution.py:151
  172.0 4.6 %fusion.13 = bf16[16,256,256]{2,1,0:T(8,128)(2,1)S(1)} fusion(f32[256,16,256]{2,0,1:T(8,128)S(1)} %fusion.3, bf16[256,768,1]{0,1,2:T(8,128)(2,1)S(1)} %bitcast.107, bf16[16,2,256,768]{3,2,1,0:T(8,128)(2,1)} %bitcast.103), kind=kOutput, calls=%fused_computation.31 | convolution fusion | flops 1612709888 | bytes 12976128 | tf_op jit(solution)/shard_map/dot_general | solution.py:146
  178.7 6.9 %all-to-all-start.1 = ((bf16[16,256,256]{2,1,0:T(8,128)(2,1)}), bf16[16,256,256]{2,1,0:T(8,128)(2,1)S(1)}, u32[]{:S(2)}, u32[]{:S(2)}) async-start(bf16[16,256,256]{2,1,0:T(8,128)(2,1)} %gather_fusion.3), calls=%async_computation.1 | async-start | bytes 4194304 | tf_op jit(solution)/shard_map/all_to_all | solution.py:160
  185.6 2.6 convolution_convert_fusion
  188.9 42.2 %all-to-all-done.1 = bf16[16,256,256]{2,1,0:T(8,128)(2,1)S(1)} async-done(((bf16[16,256,256]{2,1,0:T(8,128)(2,1)}), bf16[16,256,256]{2,1,0:T(8,128)(2,1)S(1)}, u32[]{:S(2)}, u32[]{:S(2)}) %all-to-all-start.1) | async-done | bytes 2097184 | tf_op jit(solution)/shard_map/all_to_all | solution.py:160
  232.1 13.8 %all-gather.5.cloned.1.call-done = bf16[16,256,768]{2,1,0:T(8,128)(2,1)} async-done(((bf16[1,256,768]{2,1,0:T(8,128)(2,1)}), bf16[16,256,768]{2,1,0:T(8,128)(2,1)}) %all-gather.5.cloned.1.call-update) | async-done | bytes 6291472 | tf_op jit(solution)/shard_map/all_gather | solution.py:162
  245.9 7.5 %bitcast_convert_fusion = bf16[512,768]{1,0:T(8,128)(2,1)S(1)} fusion(bf16[16,256,512]{2,1,0:T(8,128)(2,1)} %bitcast.98, bf16[16,256,768]{2,1,0:T(8,128)(2,1)} %all-gather.5.cloned.1.call-done), kind=kOutput, calls=%fused_computation.36 | convolution fusion | flops 3221618688 | bytes 11272192 | tf_op jit(solution)/shard_map/dot_general | solution.py:163
  (75 shorter events, 30.0 us)
Async XLA Ops:
  7.2 104.3 %all-gather.3.cloned.1.call-start = ((), (), s32[]{:S(2)}) async-start(), calls=%async_computation.2 | async-start | bytes 13369344 | tf_op jit(solution)/shard_map/all_gather | solution.py:66
  16.4 7.8 %copy-start.8 = (s32[32]{0:T(128)S(1)}, s32[32]{0:T(128)}, u32[]{:S(2)}) copy-start(s32[32]{0:T(128)} %param.13) | copy-start | bytes 388
  16.4 8.0 %copy-start.7 = (s32[16]{0:T(128)S(1)}, s32[16]{0:T(128)}, u32[]{:S(2)}) copy-start(s32[16]{0:T(128)} %constant.77.clone) | copy-start | bytes 196
  16.4 51.9 %all-to-all-start = ((bf16[256,16,256]{2,0,1:T(8,128)(2,1)}), bf16[256,16,256]{2,0,1:T(8,128)(2,1)}, u32[]{:S(2)}, u32[]{:S(2)}) async-start(bf16[256,16,256]{2,0,1:T(8,128)(2,1)} %copy.78), calls=%async_computation | async-start | bytes 4194304 | tf_op jit(solution)/shard_map/all_to_all | solution.py:69
  24.1 221.8 %all-gather.5.cloned.1.call-start = ((), (), s32[]{:S(2)}) async-start(), calls=%async_computation.3 | async-start | bytes 6684672 | tf_op jit(solution)/shard_map/all_gather | solution.py:162
  30.3 6.4 %copy-start.5 = (s32[4096]{0:T(1024)S(1)}, s32[4096]{0:T(1024)}, u32[]{:S(2)}) copy-start(s32[4096]{0:T(1024)} %param.14) | copy-start | bytes 49156
  30.4 6.5 %copy-start.4 = (bf16[256,256]{1,0:T(8,128)(2,1)S(1)}, bf16[256,256]{1,0:T(8,128)(2,1)}, u32[]{:S(2)}) copy-start(bf16[256,256]{1,0:T(8,128)(2,1)} %param.15) | copy-start | bytes 393220
  118.6 19.4 %collective-permute-start = (bf16[256,2,2,128]{3,0,2,1:T(8,128)(2,1)S(1)}, bf16[256,2,2,128]{3,0,2,1:T(8,128)(2,1)S(1)}, u32[]{:S(2)}, u32[]{:S(2)}) collective-permute-start(bf16[256,2,2,128]{3,0,2,1:T(8,128)(2,1)S(1)} %copy.81), channel_id=1, source_target_pairs={{0,64},{16,80},{32,96},{48,112},{64,128},{80,144},{96,160},{112,17... | collective-permute-start | bytes 786440 | tf_op jit(solution)/shard_map/ppermute | solution.py:14
  120.1 18.0 %collective-permute-start.1 = (bf16[256,2,2,128]{3,0,2,1:T(8,128)(2,1)S(1)}, bf16[256,2,2,128]{3,0,2,1:T(8,128)(2,1)S(1)}, u32[]{:S(2)}, u32[]{:S(2)}) collective-permute-start(bf16[256,2,2,128]{3,0,2,1:T(8,128)(2,1)S(1)} %copy.81), channel_id=1, source_target_pairs={{0,48},{16,64},{32,80},{48,96},{64,112},{80,128},{96,144},{112,160... | collective-permute-start | bytes 786440 | tf_op jit(solution)/shard_map/ppermute | solution.py:14
  123.3 14.8 %collective-permute-start.2 = (bf16[256,2,2,128]{3,0,2,1:T(8,128)(2,1)S(1)}, bf16[256,2,2,128]{3,0,2,1:T(8,128)(2,1)S(1)}, u32[]{:S(2)}, u32[]{:S(2)}) collective-permute-start(bf16[256,2,2,128]{3,0,2,1:T(8,128)(2,1)S(1)} %copy.81), channel_id=1, source_target_pairs={{0,32},{16,48},{32,64},{48,80},{64,96},{80,112},{96,128},{112,144}... | collective-permute-start | bytes 786440 | tf_op jit(solution)/shard_map/ppermute | solution.py:14
  128.1 10.1 %collective-permute-start.3 = (bf16[256,2,2,128]{3,0,2,1:T(8,128)(2,1)S(1)}, bf16[256,2,2,128]{3,0,2,1:T(8,128)(2,1)S(1)}, u32[]{:S(2)}, u32[]{:S(2)}) collective-permute-start(bf16[256,2,2,128]{3,0,2,1:T(8,128)(2,1)S(1)} %copy.81), channel_id=1, source_target_pairs={{0,16},{16,32},{32,48},{48,64},{64,80},{80,96},{96,112},{112,128},... | collective-permute-start | bytes 786440 | tf_op jit(solution)/shard_map/ppermute | solution.py:14
  138.3 1.0 copy-start.1
  141.9 2.6 %copy-start = (f32[2,256,1280]{2,1,0:T(8,128)}, f32[2,256,1280]{2,1,0:T(8,128)S(1)}, u32[]{:S(2)}) copy-start(f32[2,256,1280]{2,1,0:T(8,128)S(1)} %get-tuple-element.33) | copy-start | bytes 7864324
  145.3 6.5 %copy-start.2 = (bf16[1280,2,2,128]{3,0,2,1:T(8,128)(2,1)S(1)}, bf16[1280,2,2,128]{3,0,2,1:T(8,128)(2,1)}, u32[]{:S(2)}) copy-start(bf16[1280,2,2,128]{3,0,2,1:T(8,128)(2,1)} %copy-done.1) | copy-start | bytes 3932164
  145.6 9.5 %collective-permute-start.7 = (bf16[256,2,2,128]{0,3,2,1:T(8,128)(2,1)S(1)}, bf16[256,2,2,128]{0,3,2,1:T(8,128)(2,1)S(1)}, u32[]{:S(2)}, u32[]{:S(2)}) collective-permute-start(bf16[256,2,2,128]{0,3,2,1:T(8,128)(2,1)S(1)} %get-tuple-element.29), channel_id=1, source_target_pairs={{64,0},{80,16},{96,32},{112,48},{128,64},{144,80},{160,96},{176,11... | collective-permute-start | bytes 786440 | tf_op jit(solution)/shard_map/ppermute | solution.py:14
  147.1 19.0 %collective-permute-start.6 = (bf16[256,2,2,128]{0,3,2,1:T(8,128)(2,1)S(1)}, bf16[256,2,2,128]{0,3,2,1:T(8,128)(2,1)S(1)}, u32[]{:S(2)}, u32[]{:S(2)}) collective-permute-start(bf16[256,2,2,128]{0,3,2,1:T(8,128)(2,1)S(1)} %get-tuple-element.30), channel_id=1, source_target_pairs={{48,0},{64,16},{80,32},{96,48},{112,64},{128,80},{144,96},{160,112... | collective-permute-start | bytes 786440 | tf_op jit(solution)/shard_map/ppermute | solution.py:14
  148.4 17.7 %collective-permute-start.5 = (bf16[256,2,2,128]{0,3,2,1:T(8,128)(2,1)S(1)}, bf16[256,2,2,128]{0,3,2,1:T(8,128)(2,1)S(1)}, u32[]{:S(2)}, u32[]{:S(2)}) collective-permute-start(bf16[256,2,2,128]{0,3,2,1:T(8,128)(2,1)S(1)} %get-tuple-element.31), channel_id=1, source_target_pairs={{32,0},{48,16},{64,32},{80,48},{96,64},{112,80},{128,96},{144,112}... | collective-permute-start | bytes 786440 | tf_op jit(solution)/shard_map/ppermute | solution.py:14
  149.7 16.4 %collective-permute-start.4 = (bf16[256,2,2,128]{0,3,2,1:T(8,128)(2,1)S(1)}, bf16[256,2,2,128]{0,3,2,1:T(8,128)(2,1)S(1)}, u32[]{:S(2)}, u32[]{:S(2)}) collective-permute-start(bf16[256,2,2,128]{0,3,2,1:T(8,128)(2,1)S(1)} %get-tuple-element.28), channel_id=1, source_target_pairs={{16,0},{32,16},{48,32},{64,48},{80,64},{96,80},{112,96},{128,112},... | collective-permute-start | bytes 786440 | tf_op jit(solution)/shard_map/ppermute | solution.py:14
  166.3 1.0 copy-start.6
  178.7 6.9 %copy-start.3 = (bf16[1280,2,2,128]{3,0,2,1:T(8,128)(2,1)S(1)}, bf16[1280,2,2,128]{3,0,2,1:T(8,128)(2,1)}, u32[]{:S(2)}) copy-start(bf16[1280,2,2,128]{3,0,2,1:T(8,128)(2,1)} %copy-done.1) | copy-start | bytes 3932164
  178.7 52.5 %all-to-all-start.1 = ((bf16[16,256,256]{2,1,0:T(8,128)(2,1)}), bf16[16,256,256]{2,1,0:T(8,128)(2,1)S(1)}, u32[]{:S(2)}, u32[]{:S(2)}) async-start(bf16[16,256,256]{2,1,0:T(8,128)(2,1)} %gather_fusion.3), calls=%async_computation.1 | async-start | bytes 4194304 | tf_op jit(solution)/shard_map/all_to_all | solution.py:160
Sparse Core Ops, SparseCore 0:
  10.8 100.6 all-gather.2
  167.4 78.4 all-gather.4
where the time goes:
time: 263 us; the launch traced here: 262 us
  waiting for transfers between devices  137 us (52%)
  matrix products  37.7 us (14%)
  starting transfers between devices  35 us (13%)
  local copies, waits for them, and re-layouts  28.7 us (11%)
  between operations  14.5 us (6%)
  other arithmetic  9.41 us (4%)
    all_to_all x1, waiting for transfers between devices, on_device(): lax.all_to_all(parts, 'mp', split_axis=0, concat_axis=0, tiled=True)  42.2 us
    all_gather x1, waiting for transfers between devices, on_device(): lax.all_gather(flat_weights, 'dp', axis=0, tiled=True, axis_index_groups=...  36.4 us
    all_to_all x1, waiting for transfers between devices, on_device(): lax.all_to_all(tokens, 'dp', split_axis=1, concat_axis=0, tiled=True)  30.9 us
    ppermute x8, starting transfers between devices, shifted(): return lax.ppermute(block, axis, route)  20.3 us
    all_gather x1, waiting for transfers between devices, on_device(): lax.all_gather(dqkv[None], 'dp', axis=0, tiled=True, axis_index_groups=[r...  13.8 us
    ppermute x8, waiting for transfers between devices, shifted(): return lax.ppermute(block, axis, route)  13.7 us
    unnamed x27, local copies, waits for them, and re-layouts  9.27 us
    all_to_all x1, starting transfers between devices, on_device(): lax.all_to_all(tokens, 'dp', split_axis=1, concat_axis=0, tiled=True)  7.75 us
  transfers between devices with their start and end apart: 12, of which 6 were waited for; matrix products, arithmetic and copies ran while one was open for 18% of the time, Pallas kernels for 0%

commit v1 on v0

--- a/solution.py
+++ b/solution.py
@@ -66,7 +66,10 @@
     stacked_weights = lax.all_gather(
         flat_weights, "dp", axis=0, tiled=True, axis_index_groups=[ring]
     )
-    columns = lax.all_to_all(tokens, "dp", split_axis=1, concat_axis=0, tiled=True)
+    columns = jnp.concatenate(
+        lax.all_to_all(jnp.stack(jnp.split(tokens, lax.axis_size("dp"), axis=1)), "dp", 0, 0),
+        axis=0,
+    )
     ring_columns = split_by_modality_major(
         ring_blocks(columns, ring, 0), ring_blocks(token_image, ring, 0)
     )

time: 263 us -> 263 us (level)
  local copies, waits for them, and re-layouts: 28.7 us -> 40.1 us
  waiting for transfers between devices: 137 us -> 126 us
    unnamed x27 -> x44, local copies, waits for them, and re-layouts: 9.27 us -> 18.7 us
    all_to_all x1, waiting for transfers between devices: 30.9 us -> 24.9 us  [on_device(): lax.all_to_all(jnp.stack(jnp.split(tokens, lax.axis_size('dp'), axis=1)),...]
    all_gather x1, waiting for transfers between devices: 36.4 us -> 31.3 us  [on_device(): lax.all_gather(flat_weights, 'dp', axis=0, tiled=True, axis_index_groups=...]
    reshape x0 -> x1, local copies, waits for them, and re-layouts: none -> 3.99 us  [ring_blocks(): rows.reshape(shape[:axis] + (len(ring), shape[axis] // len(ring)) + shape...]
  transfers between devices with their start and end apart: 12 -> 12, of which waited for: 6 -> 6; matrix products, arithmetic and copies ran while one was open for 18% -> 22% of each run, Pallas kernels for 0% -> 0%
where the time goes in v1:
time: 263 us; the launch traced here: 262 us
  waiting for transfers between devices  126 us (48%)
  local copies, waits for them, and re-layouts  40.1 us (15%)
  matrix products  37.7 us (14%)
  starting transfers between devices  34.9 us (13%)
  between operations  14.5 us (6%)
  other arithmetic  9.41 us (4%)
    all_to_all x1, waiting for transfers between devices, on_device(): lax.all_to_all(parts, 'mp', split_axis=0, concat_axis=0, tiled=True)  42.2 us
    all_gather x1, waiting for transfers between devices, on_device(): lax.all_gather(flat_weights, 'dp', axis=0, tiled=True, axis_index_groups=...  31.3 us
    all_to_all x1, waiting for transfers between devices, on_device(): lax.all_to_all(jnp.stack(jnp.split(tokens, lax.axis_size('dp'), axis=1)),...  24.9 us
    ppermute x8, starting transfers between devices, shifted(): return lax.ppermute(block, axis, route)  20.3 us
    unnamed x44, local copies, waits for them, and re-layouts  18.7 us
    all_gather x1, waiting for transfers between devices, on_device(): lax.all_gather(dqkv[None], 'dp', axis=0, tiled=True, axis_index_groups=[r...  13.8 us
    ppermute x8, waiting for transfers between devices, shifted(): return lax.ppermute(block, axis, route)  13.7 us
    all_to_all x1, starting transfers between devices, on_device(): lax.all_to_all(jnp.stack(jnp.split(tokens, lax.axis_size('dp'), axis=1)),...  7.62 us
  transfers between devices with their start and end apart: 12, of which 6 were waited for; matrix products, arithmetic and copies ran while one was open for 22% of the time, Pallas kernels for 0%

profile of v1, /device:TPU:97, one launch (start us, length us, event | category | flops | bytes accessed | tf_op | source)
XLA Modules:
  0.0 262.5 jit_solution(14459390521832753031)
XLA Ops:
  7.2 2.4 copy.74
  21.4 7.6 %all-to-all-start = ((bf16[16,256,256]{2,1,0:T(8,128)(2,1)}), bf16[16,256,256]{2,1,0:T(8,128)(2,1)}, u32[]{:S(2)}, u32[]{:S(2)}) async-start(bf16[16,256,256]{2,1,0:T(8,128)(2,1)} %bitcast_dynamic-update-slice_fusion), calls=%async_computation | async-start | bytes 4194304 | tf_op jit(solution)/shard_map/all_to_all | solution.py:70
  29.1 2.5 copy.76
  32.5 4.0 %copy.77 = bf16[256,16,256]{2,0,1:T(8,128)(2,1)} copy(bf16[256,16,256]{0,2,1:T(8,128)(2,1)} %bitcast.128) | data formatting | bytes 4194304 | tf_op jit(solution)/shard_map/reshape | solution.py:41
  41.6 6.4 %copy.78 = bf16[256,16,2,256]{0,3,2,1:T(8,128)(2,1)} copy(bf16[256,16,2,256]{3,0,1,2:T(8,128)(2,1)} %pad_maximum_fusion.1) | data formatting | bytes 8388608 | tf_op jit(solution)/shard_map/concatenate | solution.py:77
  48.6 24.9 %all-to-all-done = bf16[16,256,256]{2,1,0:T(8,128)(2,1)} async-done(((bf16[16,256,256]{2,1,0:T(8,128)(2,1)}), bf16[16,256,256]{2,1,0:T(8,128)(2,1)}, u32[]{:S(2)}, u32[]{:S(2)}) %all-to-all-start) | async-done | bytes 2097184 | tf_op jit(solution)/shard_map/all_to_all | solution.py:70
  73.5 2.3 gather_fusion.2
  78.0 2.4 pad_maximum_fusion
  80.4 31.3 %all-gather.3.cloned.1.call-done = bf16[8192,768]{1,0:T(8,128)(2,1)} async-done(((bf16[512,768]{1,0:T(8,128)(2,1)}), bf16[8192,768]{1,0:T(8,128)(2,1)}) %all-gather.3.cloned.1.call-update) | async-done | bytes 12582928 | tf_op jit(solution)/shard_map/all_gather | solution.py:66
  111.6 7.0 %fusion.15 = bf16[256,512]{1,0:T(8,128)(2,1)S(1)} fusion(bf16[256,8192]{0,1:T(8,128)(2,1)} %bitcast.130, bf16[8192,768]{1,0:T(8,128)(2,1)} %all-gather.3.cloned.1.call-done), kind=kOutput, calls=%fused_computation.40 | convolution fusion | flops 2147614720 | bytes 12845056 | tf_op jit(solution)/shard_map/dot_general | solution.py:89
  120.2 3.2 %collective-permute-start.1 = (bf16[256,2,2,128]{3,0,2,1:T(8,128)(2,1)S(1)}, bf16[256,2,2,128]{3,0,2,1:T(8,128)(2,1)S(1)}, u32[]{:S(2)}, u32[]{:S(2)}) collective-permute-start(bf16[256,2,2,128]{3,0,2,1:T(8,128)(2,1)S(1)} %copy.79), channel_id=1, source_target_pairs={{0,48},{16,64},{32,80},{48,96},{64,112},{80,128},{96,144},{112,160... | collective-permute-start | bytes 786440 | tf_op jit(solution)/shard_map/ppermute | solution.py:14
  123.4 4.8 %collective-permute-start.2 = (bf16[256,2,2,128]{3,0,2,1:T(8,128)(2,1)S(1)}, bf16[256,2,2,128]{3,0,2,1:T(8,128)(2,1)S(1)}, u32[]{:S(2)}, u32[]{:S(2)}) collective-permute-start(bf16[256,2,2,128]{3,0,2,1:T(8,128)(2,1)S(1)} %copy.79), channel_id=1, source_target_pairs={{0,32},{16,48},{32,64},{48,80},{64,96},{80,112},{96,128},{112,144}... | collective-permute-start | bytes 786440 | tf_op jit(solution)/shard_map/ppermute | solution.py:14
  128.2 4.9 %collective-permute-start.3 = (bf16[256,2,2,128]{3,0,2,1:T(8,128)(2,1)S(1)}, bf16[256,2,2,128]{3,0,2,1:T(8,128)(2,1)S(1)}, u32[]{:S(2)}, u32[]{:S(2)}) collective-permute-start(bf16[256,2,2,128]{3,0,2,1:T(8,128)(2,1)S(1)} %copy.79), channel_id=1, source_target_pairs={{0,16},{16,32},{32,48},{48,64},{64,80},{80,96},{96,112},{112,128},... | collective-permute-start | bytes 786440 | tf_op jit(solution)/shard_map/ppermute | solution.py:14
  133.1 5.2 %fusion.19 = bf16[256,256]{0,1:T(8,128)(2,1)S(1)} fusion(bf16[256,8192]{0,1:T(8,128)(2,1)} %bitcast.131, bf16[8192,768]{1,0:T(8,128)(2,1)} %all-gather.3.cloned.1.call-done), kind=kOutput, calls=%fused_computation.43 | convolution fusion | flops 1073807360 | bytes 8519680 | tf_op jit(solution)/shard_map/dot_general | solution.py:97
  139.6 2.6 fusion.33
  152.5 2.7 %collective-permute-done.7 = bf16[256,2,2,128]{0,3,2,1:T(8,128)(2,1)S(1)} collective-permute-done((bf16[256,2,2,128]{0,3,2,1:T(8,128)(2,1)S(1)}, bf16[256,2,2,128]{0,3,2,1:T(8,128)(2,1)S(1)}, u32[]{:S(2)}, u32[]{:S(2)}) %collective-permute-start.7) | collective-permute-done | bytes 262176 | tf_op jit(solution)/shard_map/ppermute | solution.py:14
  155.3 10.9 %collective-permute-done.6 = bf16[256,2,2,128]{0,3,2,1:T(8,128)(2,1)S(1)} collective-permute-done((bf16[256,2,2,128]{0,3,2,1:T(8,128)(2,1)S(1)}, bf16[256,2,2,128]{0,3,2,1:T(8,128)(2,1)S(1)}, u32[]{:S(2)}, u32[]{:S(2)}) %collective-permute-start.6) | collective-permute-done | bytes 262176 | tf_op jit(solution)/shard_map/ppermute | solution.py:14
  167.5 4.6 %fusion.3 = f32[256,16,256]{2,0,1:T(8,128)S(1)} fusion(bf16[256,768,1]{0,1,2:T(8,128)(2,1)S(1)} %bitcast.140, bf16[16,2,256,768]{3,2,1,0:T(8,128)(2,1)} %bitcast.133), kind=kOutput, calls=%fused_computation.8 | convolution fusion | flops 1610612736 | bytes 10878976 | tf_op jit(solution)/shard_map/dot_general | solution.py:154
  172.1 4.6 %fusion.13 = bf16[16,256,256]{2,1,0:T(8,128)(2,1)S(1)} fusion(f32[256,16,256]{2,0,1:T(8,128)S(1)} %fusion.3, bf16[256,768,1]{0,1,2:T(8,128)(2,1)S(1)} %bitcast.138, bf16[16,2,256,768]{3,2,1,0:T(8,128)(2,1)} %bitcast.134), kind=kOutput, calls=%fused_computation.31 | convolution fusion | flops 1612709888 | bytes 12976128 | tf_op jit(solution)/shard_map/dot_general | solution.py:149
  178.8 6.9 %all-to-all-start.1 = ((bf16[16,256,256]{2,1,0:T(8,128)(2,1)}), bf16[16,256,256]{2,1,0:T(8,128)(2,1)S(1)}, u32[]{:S(2)}, u32[]{:S(2)}) async-start(bf16[16,256,256]{2,1,0:T(8,128)(2,1)} %gather_fusion.3), calls=%async_computation.1 | async-start | bytes 4194304 | tf_op jit(solution)/shard_map/all_to_all | solution.py:163
  185.7 2.6 convolution_convert_fusion
  189.0 42.2 %all-to-all-done.1 = bf16[16,256,256]{2,1,0:T(8,128)(2,1)S(1)} async-done(((bf16[16,256,256]{2,1,0:T(8,128)(2,1)}), bf16[16,256,256]{2,1,0:T(8,128)(2,1)S(1)}, u32[]{:S(2)}, u32[]{:S(2)}) %all-to-all-start.1) | async-done | bytes 2097184 | tf_op jit(solution)/shard_map/all_to_all | solution.py:163
  232.2 13.8 %all-gather.5.cloned.1.call-done = bf16[16,256,768]{2,1,0:T(8,128)(2,1)} async-done(((bf16[1,256,768]{2,1,0:T(8,128)(2,1)}), bf16[16,256,768]{2,1,0:T(8,128)(2,1)}) %all-gather.5.cloned.1.call-update) | async-done | bytes 6291472 | tf_op jit(solution)/shard_map/all_gather | solution.py:165
  246.0 7.5 %bitcast_convert_fusion = bf16[512,768]{1,0:T(8,128)(2,1)S(1)} fusion(bf16[16,256,512]{2,1,0:T(8,128)(2,1)} %bitcast.129, bf16[16,256,768]{2,1,0:T(8,128)(2,1)} %all-gather.5.cloned.1.call-done), kind=kOutput, calls=%fused_computation.36 | convolution fusion | flops 3221618688 | bytes 11272192 | tf_op jit(solution)/shard_map/dot_general | solution.py:166
  (93 shorter events, 40.5 us)
Async XLA Ops:
  7.2 3.6 %copy-start = (bf16[256,4096]{1,0:T(8,128)(2,1)S(1)}, bf16[256,4096]{1,0:T(8,128)(2,1)}, u32[]{:S(2)}) copy-start(bf16[256,4096]{1,0:T(8,128)(2,1)} %param.11) | copy-start | bytes 6291460
  7.2 104.5 %all-gather.3.cloned.1.call-start = ((), (), s32[]{:S(2)}) async-start(), calls=%async_computation.2 | async-start | bytes 13369344 | tf_op jit(solution)/shard_map/all_gather | solution.py:66
  21.4 52.1 %all-to-all-start = ((bf16[16,256,256]{2,1,0:T(8,128)(2,1)}), bf16[16,256,256]{2,1,0:T(8,128)(2,1)}, u32[]{:S(2)}, u32[]{:S(2)}) async-start(bf16[16,256,256]{2,1,0:T(8,128)(2,1)} %bitcast_dynamic-update-slice_fusion), calls=%async_computation | async-start | bytes 4194304 | tf_op jit(solution)/shard_map/all_to_all | solution.py:70
  29.1 2.6 copy-start.9
  29.1 2.8 %copy-start.8 = (s32[16]{0:T(128)S(1)}, s32[16]{0:T(128)}, u32[]{:S(2)}) copy-start(s32[16]{0:T(128)} %constant.77.clone) | copy-start | bytes 196
  29.1 217.0 %all-gather.5.cloned.1.call-start = ((), (), s32[]{:S(2)}) async-start(), calls=%async_computation.3 | async-start | bytes 6684672 | tf_op jit(solution)/shard_map/all_gather | solution.py:165
  41.6 6.4 %copy-start.6 = (s32[4096]{0:T(1024)S(1)}, s32[4096]{0:T(1024)}, u32[]{:S(2)}) copy-start(s32[4096]{0:T(1024)} %param.14) | copy-start | bytes 49156
  41.6 6.5 %copy-start.5 = (bf16[256,256]{1,0:T(8,128)(2,1)S(1)}, bf16[256,256]{1,0:T(8,128)(2,1)}, u32[]{:S(2)}) copy-start(bf16[256,256]{1,0:T(8,128)(2,1)} %param.15) | copy-start | bytes 393220
  118.8 19.6 %collective-permute-start = (bf16[256,2,2,128]{3,0,2,1:T(8,128)(2,1)S(1)}, bf16[256,2,2,128]{3,0,2,1:T(8,128)(2,1)S(1)}, u32[]{:S(2)}, u32[]{:S(2)}) collective-permute-start(bf16[256,2,2,128]{3,0,2,1:T(8,128)(2,1)S(1)} %copy.79), channel_id=1, source_target_pairs={{0,64},{16,80},{32,96},{48,112},{64,128},{80,144},{96,160},{112,17... | collective-permute-start | bytes 786440 | tf_op jit(solution)/shard_map/ppermute | solution.py:14
  120.2 18.2 %collective-permute-start.1 = (bf16[256,2,2,128]{3,0,2,1:T(8,128)(2,1)S(1)}, bf16[256,2,2,128]{3,0,2,1:T(8,128)(2,1)S(1)}, u32[]{:S(2)}, u32[]{:S(2)}) collective-permute-start(bf16[256,2,2,128]{3,0,2,1:T(8,128)(2,1)S(1)} %copy.79), channel_id=1, source_target_pairs={{0,48},{16,64},{32,80},{48,96},{64,112},{80,128},{96,144},{112,160... | collective-permute-start | bytes 786440 | tf_op jit(solution)/shard_map/ppermute | solution.py:14
  123.4 15.0 %collective-permute-start.2 = (bf16[256,2,2,128]{3,0,2,1:T(8,128)(2,1)S(1)}, bf16[256,2,2,128]{3,0,2,1:T(8,128)(2,1)S(1)}, u32[]{:S(2)}, u32[]{:S(2)}) collective-permute-start(bf16[256,2,2,128]{3,0,2,1:T(8,128)(2,1)S(1)} %copy.79), channel_id=1, source_target_pairs={{0,32},{16,48},{32,64},{48,80},{64,96},{80,112},{96,128},{112,144}... | collective-permute-start | bytes 786440 | tf_op jit(solution)/shard_map/ppermute | solution.py:14
  128.2 10.3 %collective-permute-start.3 = (bf16[256,2,2,128]{3,0,2,1:T(8,128)(2,1)S(1)}, bf16[256,2,2,128]{3,0,2,1:T(8,128)(2,1)S(1)}, u32[]{:S(2)}, u32[]{:S(2)}) collective-permute-start(bf16[256,2,2,128]{3,0,2,1:T(8,128)(2,1)S(1)} %copy.79), channel_id=1, source_target_pairs={{0,16},{16,32},{32,48},{48,64},{64,80},{80,96},{96,112},{112,128},... | collective-permute-start | bytes 786440 | tf_op jit(solution)/shard_map/ppermute | solution.py:14
  138.6 1.0 copy-start.2
  142.2 2.6 %copy-start.1 = (f32[2,256,1280]{2,1,0:T(8,128)}, f32[2,256,1280]{2,1,0:T(8,128)S(1)}, u32[]{:S(2)}) copy-start(f32[2,256,1280]{2,1,0:T(8,128)S(1)} %get-tuple-element.33) | copy-start | bytes 7864324
  145.6 6.3 %copy-start.3 = (bf16[1280,2,2,128]{3,0,2,1:T(8,128)(2,1)S(1)}, bf16[1280,2,2,128]{3,0,2,1:T(8,128)(2,1)}, u32[]{:S(2)}) copy-start(bf16[1280,2,2,128]{3,0,2,1:T(8,128)(2,1)} %copy-done.2) | copy-start | bytes 3932164
  146.0 9.3 %collective-permute-start.7 = (bf16[256,2,2,128]{0,3,2,1:T(8,128)(2,1)S(1)}, bf16[256,2,2,128]{0,3,2,1:T(8,128)(2,1)S(1)}, u32[]{:S(2)}, u32[]{:S(2)}) collective-permute-start(bf16[256,2,2,128]{0,3,2,1:T(8,128)(2,1)S(1)} %get-tuple-element.29), channel_id=1, source_target_pairs={{64,0},{80,16},{96,32},{112,48},{128,64},{144,80},{160,96},{176,11... | collective-permute-start | bytes 786440 | tf_op jit(solution)/shard_map/ppermute | solution.py:14
  147.4 18.8 %collective-permute-start.6 = (bf16[256,2,2,128]{0,3,2,1:T(8,128)(2,1)S(1)}, bf16[256,2,2,128]{0,3,2,1:T(8,128)(2,1)S(1)}, u32[]{:S(2)}, u32[]{:S(2)}) collective-permute-start(bf16[256,2,2,128]{0,3,2,1:T(8,128)(2,1)S(1)} %get-tuple-element.30), channel_id=1, source_target_pairs={{48,0},{64,16},{80,32},{96,48},{112,64},{128,80},{144,96},{160,112... | collective-permute-start | bytes 786440 | tf_op jit(solution)/shard_map/ppermute | solution.py:14
  148.7 17.5 %collective-permute-start.5 = (bf16[256,2,2,128]{0,3,2,1:T(8,128)(2,1)S(1)}, bf16[256,2,2,128]{0,3,2,1:T(8,128)(2,1)S(1)}, u32[]{:S(2)}, u32[]{:S(2)}) collective-permute-start(bf16[256,2,2,128]{0,3,2,1:T(8,128)(2,1)S(1)} %get-tuple-element.31), channel_id=1, source_target_pairs={{32,0},{48,16},{64,32},{80,48},{96,64},{112,80},{128,96},{144,112}... | collective-permute-start | bytes 786440 | tf_op jit(solution)/shard_map/ppermute | solution.py:14
  150.0 16.2 %collective-permute-start.4 = (bf16[256,2,2,128]{0,3,2,1:T(8,128)(2,1)S(1)}, bf16[256,2,2,128]{0,3,2,1:T(8,128)(2,1)S(1)}, u32[]{:S(2)}, u32[]{:S(2)}) collective-permute-start(bf16[256,2,2,128]{0,3,2,1:T(8,128)(2,1)S(1)} %get-tuple-element.28), channel_id=1, source_target_pairs={{16,0},{32,16},{48,32},{64,48},{80,64},{96,80},{112,96},{128,112},... | collective-permute-start | bytes 786440 | tf_op jit(solution)/shard_map/ppermute | solution.py:14
  166.4 1.0 copy-start.7
  178.8 6.9 %copy-start.4 = (bf16[1280,2,2,128]{3,0,2,1:T(8,128)(2,1)S(1)}, bf16[1280,2,2,128]{3,0,2,1:T(8,128)(2,1)}, u32[]{:S(2)}) copy-start(bf16[1280,2,2,128]{3,0,2,1:T(8,128)(2,1)} %copy-done.2) | copy-start | bytes 3932164
  178.8 52.5 %all-to-all-start.1 = ((bf16[16,256,256]{2,1,0:T(8,128)(2,1)}), bf16[16,256,256]{2,1,0:T(8,128)(2,1)S(1)}, u32[]{:S(2)}, u32[]{:S(2)}) async-start(bf16[16,256,256]{2,1,0:T(8,128)(2,1)} %gather_fusion.3), calls=%async_computation.1 | async-start | bytes 4194304 | tf_op jit(solution)/shard_map/all_to_all | solution.py:163
Sparse Core Ops, SparseCore 0:
  10.9 100.6 all-gather.2
  167.5 78.4 all-gather.4
